TPU v7x, 256 devices: a whole 4x4x8 slice. The times are simulated.
256 devices in a mesh: rep: 32 (over z, y_hi, core), tp: 8 (over x, y_lo).
Axes of the slice: x: 4, y: 4 (y_hi: 2, y_lo: 2; y = y_hi * 2 + y_lo), z: 8, core: 2. Of those that a mesh axis runs over, the one named last changes fastest.
Arguments:
- acts: bfloat16 [32, 1024, 4096], P('rep', 'tp'), may hold values from -6 to 6
- weights: bfloat16 [32, 4096, 4096], P('rep', None, 'tp'), may hold values from -6 to 6
- cotangent: bfloat16 [32, 1024, 4096], P('rep', None, 'tp'), may hold values from -6 to 6
- start_factors: float32 [4096, 32], replicated, may hold values from -6 to 6
Outputs:
- projected: bfloat16 [32, 1024, 4096], P('rep', None, 'tp')
- new_weights: bfloat16 [32, 4096, 4096], P('rep', None, 'tp')
All inputs are finite; a program needn't handle non-finite values.
Results may differ from a plain program's by a relative error of at most 0.001.
Values may be sent and summed in bfloat16 or wider, within the bound.
No kernel may reach another device: no remote copies, remote signals or barrier semaphores. Data moves between devices by JAX's collectives and lax.ppermute only.
A program may use at most 128 MiB of HBM per device.

v0:
```python
import jax
import jax.numpy as jnp
from jax import lax
from jax.sharding import PartitionSpec as P

D = 4096
STEPS = 3
HIGH = lax.Precision.HIGHEST


def partner(block, axis, stride):
    count = lax.axis_size(axis)
    route = []
    for low in range(count):
        high = low | 1 << stride
        if high != low and high < count:
            route += [(low, high), (high, low)]
    return lax.ppermute(block, axis, route)


def shards(acts, weights, cotangent, start_factors):
    scale = D ** (-0.5)
    weight_part = weights[0]
    grad_out = cotangent[0]
    projected = (
        jnp.dot(
            lax.all_gather(acts, "tp", axis=1, tiled=True)[0],
            weight_part,
            preferred_element_type=jnp.float32,
        )
        * scale
    ).astype(jnp.bfloat16)[None]
    grad = lax.dot_general(
        lax.all_gather(acts, "tp", axis=1, tiled=True)[0],
        grad_out,
        (((0,), (0,)), ((), ())),
        preferred_element_type=jnp.float32,
    )
    current = weight_part.astype(jnp.float32) - 0.5 * scale * grad
    for step in range(STEPS):
        side = lax.dot_general(current, start_factors, (((0,), (0,)), ((), ())), precision=HIGH)
        other = partner(side, "rep", step)
        diff = side - other
        gram = lax.psum(jnp.dot(diff.T, diff, precision=HIGH), "tp")
        lower = jnp.linalg.cholesky(gram)
        ortho = jax.scipy.linalg.solve_triangular(lower, diff.T, lower=True).T
        local = jnp.dot(current, ortho, precision=HIGH)
        summed = lax.psum(local, "tp")
        back = summed + partner(summed, "rep", step)
        current = current - 0.5 * jnp.dot(back, ortho.T, precision=HIGH)
    return (projected, current.astype(jnp.bfloat16)[None])


def solution(mesh):
    in_specs = (P("rep", "tp", None), P("rep", None, "tp"), P("rep", None, "tp"), P())
    out_specs = (P("rep", None, "tp"), P("rep", None, "tp"))
    return jax.shard_map(shards, mesh=mesh, in_specs=in_specs, out_specs=out_specs, check_vma=False)
```

profile of v0, /device:TPU:16, one launch (start us, length us, event | category | flops | bytes accessed | tf_op | source)
XLA Modules:
  0.0 682.2 jit_solution(12295986545836351096)
XLA Ops:
  8.0 175.2 %all-gather.2.cloned.1.call-done = bf16[1,1024,4096]{2,1,0:T(8,128)(2,1)} async-done(((bf16[1,128,4096]{2,1,0:T(8,128)(2,1)}), bf16[1,1024,4096]{2,1,0:T(8,128)(2,1)}) %all-gather.2.cloned.1.call-update) | async-done | bytes 8388624 | tf_op jit(solution)/shard_map/all_gather | solution.py:27
  183.2 12.2 %multiply_subtract_fusion.2 = f32[4096,512]{1,0:T(8,128)S(1)} fusion(bf16[1,1024,4096]{2,1,0:T(8,128)(2,1)} %all-gather.2.cloned.1.call-done, bf16[1,4096,512]{2,1,0:T(8,128)(2,1)} %param.8, bf16[1,1024,512]{2,1,0:T(8,128)(2,1)S(1)} %copy-done), kind=kOutput, calls=%fused_computation.7 | convolution fusion | flops 4301258752 | bytes 22020096 | tf_op jit(solution)/shard_map/dot_general | solution.py:33
  195.4 3.2 copy-done.3
  198.6 5.1 fusion.45
  205.2 34.0 %psum.42 = f32[32,32]{0,1:T(8,128)S(1)} all-reduce(f32[32,32]{0,1:T(8,128)S(1)} %fusion.34), channel_id=1, replica_groups=mesh['rep'=32,'tp'=8] {'tp'}, use_global_device_ids=true, to_apply=%region_0.0 | all-reduce | flops 1024 | bytes 8192 | tf_op jit(solution)/shard_map/psum | solution.py:44
  239.4 2.9 cholesky.59
  246.3 10.8 %fusion.46 = f32[4096,32]{0,1:T(8,128)} fusion(f32[4096,512]{1,0:T(8,128)} %copy-done.3, f32[32,512]{1,0:T(8,128)S(1)} %fusion.25), kind=kOutput, calls=%fused_computation.55 | convolution fusion | flops 805306368 | bytes 8978432 | tf_op jit(solution)/shard_map/dot_general | solution.py:47
  257.2 78.7 %all-reduce.4.cloned.1.call-done = f32[4096,32]{0,1:T(8,128)} async-done(((f32[4096,32]{0,1:T(8,128)}), f32[4096,32]{0,1:T(8,128)}) %all-reduce.4.cloned.1.call-update) | async-done | bytes 524304 | tf_op jit(solution)/shard_map/psum | solution.py:48
  338.0 9.4 %multiply_subtract_fusion.1 = f32[4096,512]{1,0:T(8,128)S(1)} fusion(f32[4096,512]{1,0:T(8,128)} %copy-done.3, f32[32,512]{1,0:T(8,128)S(1)} %fusion.25, f32[4096,32]{0,1:T(8,128)} %all-reduce.4.cloned.1.call-done, f32[4096,32]{0,1:T(8,128)S(1)} %collective-permute-done.1), kind=kOutput, calls=%fused_computation.6 | convolution fusion | flops 809631744 | bytes 17891328 | tf_op jit(solution)/shard_map/dot_general | solution.py:50
  347.4 3.2 copy-done.1
  350.6 5.1 fusion.47
  356.7 4.9 collective-permute-done.2
  361.8 32.4 %psum.44 = f32[32,32]{0,1:T(8,128)S(1)} all-reduce(f32[32,32]{0,1:T(8,128)S(1)} %fusion.31), channel_id=1, replica_groups=mesh['rep'=32,'tp'=8] {'tp'}, use_global_device_ids=true, to_apply=%region_4.0 | all-reduce | flops 1024 | bytes 8192 | tf_op jit(solution)/shard_map/psum | solution.py:44
  401.3 10.8 %fusion.48 = f32[4096,32]{0,1:T(8,128)} fusion(f32[4096,512]{1,0:T(8,128)} %copy-done.1, f32[32,512]{1,0:T(8,128)S(1)} %fusion.23), kind=kOutput, calls=%fused_computation.57 | convolution fusion | flops 805306368 | bytes 8978432 | tf_op jit(solution)/shard_map/dot_general | solution.py:47
  412.1 78.8 %all-reduce.6.cloned.1.call-done = f32[4096,32]{0,1:T(8,128)} async-done(((f32[4096,32]{0,1:T(8,128)}), f32[4096,32]{0,1:T(8,128)}) %all-reduce.6.cloned.1.call-update) | async-done | bytes 524304 | tf_op jit(solution)/shard_map/psum | solution.py:48
  491.8 10.0 %collective-permute-done.3 = f32[4096,32]{0,1:T(8,128)S(1)} collective-permute-done((f32[4096,32]{0,1:T(8,128)}, f32[4096,32]{0,1:T(8,128)S(1)}, u32[]{:S(2)}, u32[]{:S(2)}) %collective-permute-start.3) | collective-permute-done | bytes 524320 | tf_op jit(solution)/shard_map/ppermute | solution.py:18
  501.8 9.4 %multiply_subtract_fusion = f32[4096,512]{1,0:T(8,128)S(1)} fusion(f32[4096,512]{1,0:T(8,128)} %copy-done.1, f32[32,512]{1,0:T(8,128)S(1)} %fusion.23, f32[4096,32]{0,1:T(8,128)} %all-reduce.6.cloned.1.call-done, f32[4096,32]{0,1:T(8,128)S(1)} %collective-permute-done.3), kind=kOutput, calls=%fused_computation.5 | convolution fusion | flops 809631744 | bytes 17891328 | tf_op jit(solution)/shard_map/dot_general | solution.py:50
  511.3 3.2 copy-done.2
  514.5 5.1 fusion.49
  524.1 32.5 %psum.46 = f32[32,32]{0,1:T(8,128)S(1)} all-reduce(f32[32,32]{0,1:T(8,128)S(1)} %fusion.28), channel_id=1, replica_groups=mesh['rep'=32,'tp'=8] {'tp'}, use_global_device_ids=true, to_apply=%region_6.9 | all-reduce | flops 1024 | bytes 8192 | tf_op jit(solution)/shard_map/psum | solution.py:44
  563.6 10.8 %fusion.50 = f32[4096,32]{0,1:T(8,128)} fusion(f32[4096,512]{1,0:T(8,128)} %copy-done.2, f32[32,512]{1,0:T(8,128)S(1)} %fusion.21), kind=kOutput, calls=%fused_computation.59 | convolution fusion | flops 805306368 | bytes 8978432 | tf_op jit(solution)/shard_map/dot_general | solution.py:47
  574.4 78.8 %all-reduce.8.cloned.1.call-done = f32[4096,32]{0,1:T(8,128)} async-done(((f32[4096,32]{0,1:T(8,128)}), f32[4096,32]{0,1:T(8,128)}) %all-reduce.8.cloned.1.call-update) | async-done | bytes 524304 | tf_op jit(solution)/shard_map/psum | solution.py:48
  654.8 10.0 %fusion.12 = bf16[1,1024,512]{2,1,0:T(8,128)(2,1)} fusion(bf16[1,4096,512]{2,1,0:T(8,128)(2,1)} %param.8, bf16[1,1024,4096]{2,1,0:T(8,128)(2,1)} %all-gather.2.cloned.1.call-done), kind=kOutput, calls=%fused_computation.11 | convolution fusion | flops 4296015872 | bytes 13631488 | tf_op jit(solution)/shard_map/dot_general | solution.py:26
  664.8 10.6 %fusion.6 = bf16[1,4096,512]{2,1,0:T(8,128)(2,1)} fusion(f32[4096,512]{1,0:T(8,128)} %copy-done.2, f32[32,512]{1,0:T(8,128)S(1)} %fusion.21, f32[4096,32]{0,1:T(8,128)S(1)} %copy-done.5, f32[4096,32]{0,1:T(8,128)S(1)} %collective-permute-done.5), kind=kOutput, calls=%fused_computation.8 | convolution fusion | flops 811728896 | bytes 13697024 | tf_op jit(solution)/shard_map/dot_general | solution.py:50
  (53 shorter events, 30.9 us)
Async XLA Ops:
  7.2 176.0 %copy-start = (bf16[1,1024,512]{2,1,0:T(8,128)(2,1)S(1)}, bf16[1,1024,512]{2,1,0:T(8,128)(2,1)}, u32[]{:S(2)}) copy-start(bf16[1,1024,512]{2,1,0:T(8,128)(2,1)} %param.9) | copy-start | bytes 3145732
  7.2 176.0 %all-gather.2.cloned.1.call-start = ((), (), s32[]{:S(2)}) async-start(), calls=%async_computation | async-start | bytes 9437184 | tf_op jit(solution)/shard_map/all_gather | solution.py:27
  7.9 190.7 %copy-start.4 = (f32[4096,32]{0,1:T(8,128)S(1)}, f32[4096,32]{0,1:T(8,128)}, u32[]{:S(2)}) copy-start(f32[4096,32]{0,1:T(8,128)} %param.10) | copy-start | bytes 1572868
  7.9 328.0 %all-reduce.4.cloned.1.call-start = ((), (), s32[]{:S(2)}) async-start(), calls=%async_computation.1 | async-start | bytes 1048576 | tf_op jit(solution)/shard_map/psum | solution.py:48
  195.4 3.2 copy-start.3
  203.7 1.3 collective-permute-start
  257.1 233.8 %all-reduce.6.cloned.1.call-start = ((), (), s32[]{:S(2)}) async-start(), calls=%async_computation.2 | async-start | bytes 1048576 | tf_op jit(solution)/shard_map/psum | solution.py:48
  335.9 2.1 collective-permute-start.1
  347.4 3.2 copy-start.1
  355.7 5.9 collective-permute-start.2
  412.1 241.1 %all-reduce.8.cloned.1.call-start = ((), (), s32[]{:S(2)}) async-start(), calls=%async_computation.3 | async-start | bytes 1048576 | tf_op jit(solution)/shard_map/psum | solution.py:48
  490.9 10.9 %collective-permute-start.3 = (f32[4096,32]{0,1:T(8,128)}, f32[4096,32]{0,1:T(8,128)S(1)}, u32[]{:S(2)}, u32[]{:S(2)}) collective-permute-start(f32[4096,32]{0,1:T(8,128)} %all-reduce.6.cloned.1.call-done), channel_id=1, source_target_pairs={{0,16},{16,0},{8,24},{24,8},{32,48},{48,32},{40,56},{56,40},{64,80... | collective-permute-start | bytes 1572872 | tf_op jit(solution)/shard_map/ppermute | solution.py:18
  511.3 3.2 copy-start.2
  519.5 4.4 collective-permute-start.4
  653.2 11.6 %copy-start.5 = (f32[4096,32]{0,1:T(8,128)S(1)}, f32[4096,32]{0,1:T(8,128)}, u32[]{:S(2)}) copy-start(f32[4096,32]{0,1:T(8,128)} %all-reduce.8.cloned.1.call-done) | copy-start | bytes 1572868
  653.2 11.6 %collective-permute-start.5 = (f32[4096,32]{0,1:T(8,128)}, f32[4096,32]{0,1:T(8,128)S(1)}, u32[]{:S(2)}, u32[]{:S(2)}) collective-permute-start(f32[4096,32]{0,1:T(8,128)} %all-reduce.8.cloned.1.call-done), channel_id=1, source_target_pairs={{0,32},{32,0},{8,40},{40,8},{16,48},{48,16},{24,56},{56,24},{64,96... | collective-permute-start | bytes 1572872 | tf_op jit(solution)/shard_map/ppermute | solution.py:18
Sparse Core Ops, SparseCore 0:
  9.8 173.3 all-gather.1
  257.3 78.5 all-reduce.3
  412.2 78.7 all-reduce.5
  574.6 78.6 all-reduce.7
where the time goes:
time: 689 us; the launch traced here: 682 us
  waiting for transfers between devices  433 us (63%)
  matrix products  101 us (15%)
  blocking collectives  98.9 us (14%)
  other arithmetic  20.1 us (3%)
  between operations  14.2 us (2%)
  local copies, waits for them, and re-layouts  9.85 us (1%)
    psum x3, waiting for transfers between devices, shards(): summed = lax.psum(local, 'tp')  236 us
    all_gather x1, waiting for transfers between devices, shards(): lax.all_gather(acts, 'tp', axis=1, tiled=True)[0]  175 us
    psum x3, blocking collectives, shards(): gram = lax.psum(jnp.dot(diff.T, diff, precision=HIGH), 'tp')  98.9 us
    dot_general x3, matrix products, shards(): local = jnp.dot(current, ortho, precision=HIGH)  32.3 us
    dot_general x3, matrix products, shards(): current = current - 0.5 * jnp.dot(back, ortho.T, precision=HIGH)  29.5 us
    ppermute x6, waiting for transfers between devices, partner(): return lax.ppermute(block, axis, route)  21 us
    dot_general x3, matrix products, shards(): lax.dot_general(current, start_factors, (((0,), (0,)), ((), ())), precisi...  15.2 us
  transfers between devices with their start and end apart: 10, of which 9 were waited for; matrix products, arithmetic and copies ran while one was open for 1% of the time, Pallas kernels for 0%

commit v1 on v0

--- a/solution.py
+++ b/solution.py
@@ -24,7 +24,9 @@
     grad_out = cotangent[0]
     projected = (
         jnp.dot(
-            lax.all_gather(acts, "tp", axis=1, tiled=True)[0],
+            jnp.concatenate(
+                lax.all_to_all(jnp.stack([acts] * lax.axis_size("tp")), "tp", 0, 0), axis=1
+            )[0],
             weight_part,
             preferred_element_type=jnp.float32,
         )

time: 689 us -> 781 us (1.13)
  waiting for transfers between devices: 433 us -> 478 us
  blocking collectives: 98.9 us -> 136 us
    ppermute x6, waiting for transfers between devices: 21 us -> 66.1 us  [partner(): return lax.ppermute(block, axis, route)]
    psum x3, blocking collectives: 98.9 us -> 136 us  [shards(): gram = lax.psum(jnp.dot(diff.T, diff, precision=HIGH), 'tp')]
  transfers between devices with their start and end apart: 10 -> 11, of which waited for: 9 -> 8; matrix products, arithmetic and copies ran while one was open for 1% -> 10% of each run, Pallas kernels for 0% -> 0%
where the time goes in v1:
time: 781 us; the launch traced here: 774 us
  waiting for transfers between devices  478 us (61%)
  blocking collectives  136 us (17%)
  matrix products  101 us (13%)
  other arithmetic  20.1 us (3%)
  local copies, waits for them, and re-layouts  14.2 us (2%)
  between operations  14.2 us (2%)
  starting transfers between devices  10.9 us (1%)
    psum x3, waiting for transfers between devices, shards(): summed = lax.psum(local, 'tp')  236 us
    all_gather x1, waiting for transfers between devices, shards(): lax.all_gather(acts, 'tp', axis=1, tiled=True)[0]  175 us
    psum x3, blocking collectives, shards(): gram = lax.psum(jnp.dot(diff.T, diff, precision=HIGH), 'tp')  136 us
    ppermute x6, waiting for transfers between devices, partner(): return lax.ppermute(block, axis, route)  66.1 us
    dot_general x3, matrix products, shards(): local = jnp.dot(current, ortho, precision=HIGH)  32.3 us
    dot_general x3, matrix products, shards(): current = current - 0.5 * jnp.dot(back, ortho.T, precision=HIGH)  29.4 us
  transfers between devices with their start and end apart: 11, of which 8 were waited for; matrix products, arithmetic and copies ran while one was open for 10% of the time, Pallas kernels for 0%

profile of v1, /device:TPU:16, one launch (start us, length us, event | category | flops | bytes accessed | tf_op | source)
XLA Modules:
  0.0 773.9 jit_solution(17589106683952813086)
XLA Ops:
  8.0 175.2 %all-gather.2.cloned.1.call-done = bf16[1,1024,4096]{2,1,0:T(8,128)(2,1)} async-done(((bf16[1,128,4096]{2,1,0:T(8,128)(2,1)}), bf16[1,1024,4096]{2,1,0:T(8,128)(2,1)}) %all-gather.2.cloned.1.call-update) | async-done | bytes 8388624 | tf_op jit(solution)/shard_map/all_gather | solution.py:36
  183.2 12.2 %multiply_subtract_fusion.2 = f32[4096,512]{1,0:T(8,128)S(1)} fusion(bf16[1,1024,4096]{2,1,0:T(8,128)(2,1)} %all-gather.2.cloned.1.call-done, bf16[1,4096,512]{2,1,0:T(8,128)(2,1)} %param.8, bf16[1,1024,512]{2,1,0:T(8,128)(2,1)S(1)} %copy-done), kind=kOutput, calls=%fused_computation.5 | convolution fusion | flops 4301258752 | bytes 22020096 | tf_op jit(solution)/shard_map/dot_general | solution.py:35
  195.4 3.2 copy-done.4
  198.6 5.1 fusion.40
  205.2 33.9 %psum.42 = f32[32,32]{0,1:T(8,128)S(1)} all-reduce(f32[32,32]{0,1:T(8,128)S(1)} %fusion.29), channel_id=1, replica_groups=mesh['rep'=32,'tp'=8] {'tp'}, use_global_device_ids=true, to_apply=%region_0.0 | all-reduce | flops 1024 | bytes 8192 | tf_op jit(solution)/shard_map/psum | solution.py:46
  246.2 10.8 %fusion.41 = f32[4096,32]{0,1:T(8,128)} fusion(f32[4096,512]{1,0:T(8,128)} %copy-done.4, f32[32,512]{1,0:T(8,128)S(1)} %fusion.20), kind=kOutput, calls=%fused_computation.54 | convolution fusion | flops 805306368 | bytes 8978432 | tf_op jit(solution)/shard_map/dot_general | solution.py:49
  257.0 78.7 %all-reduce.4.cloned.1.call-done = f32[4096,32]{0,1:T(8,128)} async-done(((f32[4096,32]{0,1:T(8,128)}), f32[4096,32]{0,1:T(8,128)}) %all-reduce.4.cloned.1.call-update) | async-done | bytes 524304 | tf_op jit(solution)/shard_map/psum | solution.py:50
  335.7 4.3 stack.2
  340.0 5.1 all-to-all-start
  345.7 9.3 %multiply_subtract_fusion.1 = f32[4096,512]{1,0:T(8,128)S(1)} fusion(f32[4096,512]{1,0:T(8,128)} %copy-done.4, f32[32,512]{1,0:T(8,128)S(1)} %fusion.20, f32[4096,32]{0,1:T(8,128)S(1)} %copy-done.7, f32[4096,32]{0,1:T(8,128)S(1)} %collective-permute-done.1), kind=kOutput, calls=%fused_computation.4 | convolution fusion | flops 809631744 | bytes 17891328 | tf_op jit(solution)/shard_map/dot_general | solution.py:52
  355.0 3.2 copy-done.3
  358.2 5.1 fusion.42
  364.2 52.1 %collective-permute-done.2 = f32[512,32]{0,1:T(8,128)S(1)} collective-permute-done((f32[512,32]{0,1:T(8,128)S(1)}, f32[512,32]{0,1:T(8,128)S(1)}, u32[]{:S(2)}, u32[]{:S(2)}) %collective-permute-start.2) | collective-permute-done | bytes 65568 | tf_op jit(solution)/shard_map/ppermute | solution.py:18
  416.5 69.3 %psum.44 = f32[32,32]{0,1:T(8,128)S(1)} all-reduce(f32[32,32]{0,1:T(8,128)S(1)} %fusion.26), channel_id=1, replica_groups=mesh['rep'=32,'tp'=8] {'tp'}, use_global_device_ids=true, to_apply=%region_4.0 | all-reduce | flops 1024 | bytes 8192 | tf_op jit(solution)/shard_map/psum | solution.py:46
  492.9 10.8 %fusion.43 = f32[4096,32]{0,1:T(8,128)} fusion(f32[4096,512]{1,0:T(8,128)} %copy-done.3, f32[32,512]{1,0:T(8,128)S(1)} %fusion.18), kind=kOutput, calls=%fused_computation.56 | convolution fusion | flops 805306368 | bytes 8978432 | tf_op jit(solution)/shard_map/dot_general | solution.py:49
  503.7 78.9 %all-reduce.6.cloned.1.call-done = f32[4096,32]{0,1:T(8,128)} async-done(((f32[4096,32]{0,1:T(8,128)}), f32[4096,32]{0,1:T(8,128)}) %all-reduce.6.cloned.1.call-update) | async-done | bytes 524304 | tf_op jit(solution)/shard_map/psum | solution.py:50
  583.4 10.0 %collective-permute-done.3 = f32[4096,32]{0,1:T(8,128)S(1)} collective-permute-done((f32[4096,32]{0,1:T(8,128)}, f32[4096,32]{0,1:T(8,128)S(1)}, u32[]{:S(2)}, u32[]{:S(2)}) %collective-permute-start.3) | collective-permute-done | bytes 524320 | tf_op jit(solution)/shard_map/ppermute | solution.py:18
  593.5 9.4 %multiply_subtract_fusion = f32[4096,512]{1,0:T(8,128)S(1)} fusion(f32[4096,512]{1,0:T(8,128)} %copy-done.3, f32[32,512]{1,0:T(8,128)S(1)} %fusion.18, f32[4096,32]{0,1:T(8,128)} %all-reduce.6.cloned.1.call-done, f32[4096,32]{0,1:T(8,128)S(1)} %collective-permute-done.3), kind=kOutput, calls=%fused_computation.3 | convolution fusion | flops 809631744 | bytes 17891328 | tf_op jit(solution)/shard_map/dot_general | solution.py:52
  606.1 5.1 fusion.44
  615.7 32.5 %psum.46 = f32[32,32]{0,1:T(8,128)S(1)} all-reduce(f32[32,32]{0,1:T(8,128)S(1)} %fusion.23), channel_id=1, replica_groups=mesh['rep'=32,'tp'=8] {'tp'}, use_global_device_ids=true, to_apply=%region_6.9 | all-reduce | flops 1024 | bytes 8192 | tf_op jit(solution)/shard_map/psum | solution.py:46
  655.3 10.8 %fusion.45 = f32[4096,32]{0,1:T(8,128)} fusion(f32[4096,512]{1,0:T(8,128)} %copy-done.2, f32[32,512]{1,0:T(8,128)S(1)} %fusion.16), kind=kOutput, calls=%fused_computation.58 | convolution fusion | flops 805306368 | bytes 8978432 | tf_op jit(solution)/shard_map/dot_general | solution.py:49
  666.1 78.8 %all-reduce.8.cloned.1.call-done = f32[4096,32]{0,1:T(8,128)} async-done(((f32[4096,32]{0,1:T(8,128)}), f32[4096,32]{0,1:T(8,128)}) %all-reduce.8.cloned.1.call-update) | async-done | bytes 524304 | tf_op jit(solution)/shard_map/psum | solution.py:50
  746.4 10.1 %fusion.9 = bf16[1,1024,512]{2,1,0:T(8,128)(2,1)} fusion(bf16[1024,4096]{1,0:T(8,128)(2,1)} %bitcast.1, bf16[1,4096,512]{2,1,0:T(8,128)(2,1)} %param.8), kind=kOutput, calls=%fused_computation.10 | convolution fusion | flops 4296015872 | bytes 13631488 | tf_op jit(solution)/shard_map/dot_general | solution.py:26
  756.5 10.6 %fusion.4 = bf16[1,4096,512]{2,1,0:T(8,128)(2,1)} fusion(f32[4096,512]{1,0:T(8,128)} %copy-done.2, f32[32,512]{1,0:T(8,128)S(1)} %fusion.16, f32[4096,32]{0,1:T(8,128)S(1)} %copy-done.8, f32[4096,32]{0,1:T(8,128)S(1)} %collective-permute-done.5), kind=kOutput, calls=%fused_computation.6 | convolution fusion | flops 811728896 | bytes 13697024 | tf_op jit(solution)/shard_map/dot_general | solution.py:52
  (62 shorter events, 35.4 us)
Async XLA Ops:
  7.2 176.0 %copy-start = (bf16[1,1024,512]{2,1,0:T(8,128)(2,1)S(1)}, bf16[1,1024,512]{2,1,0:T(8,128)(2,1)}, u32[]{:S(2)}) copy-start(bf16[1,1024,512]{2,1,0:T(8,128)(2,1)} %param.9) | copy-start | bytes 3145732
  7.2 176.0 %all-gather.2.cloned.1.call-start = ((), (), s32[]{:S(2)}) async-start(), calls=%async_computation.1 | async-start | bytes 9437184 | tf_op jit(solution)/shard_map/all_gather | solution.py:36
  7.9 190.7 %copy-start.5 = (f32[4096,32]{0,1:T(8,128)S(1)}, f32[4096,32]{0,1:T(8,128)}, u32[]{:S(2)}) copy-start(f32[4096,32]{0,1:T(8,128)} %param.10) | copy-start | bytes 1572868
  7.9 327.8 %all-reduce.4.cloned.1.call-start = ((), (), s32[]{:S(2)}) async-start(), calls=%async_computation.2 | async-start | bytes 1048576 | tf_op jit(solution)/shard_map/psum | solution.py:50
  195.4 3.2 copy-start.4
  198.6 137.1 %copy-start.6 = (bf16[1,128,4096]{2,1,0:T(8,128)(2,1)S(1)}, bf16[1,128,4096]{2,1,0:T(8,128)(2,1)}, u32[]{:S(2)}) copy-start(bf16[1,128,4096]{2,1,0:T(8,128)(2,1)} %param.7) | copy-start | bytes 3145732
  203.7 1.3 collective-permute-start
  335.7 9.9 %collective-permute-start.1 = (f32[4096,32]{0,1:T(8,128)}, f32[4096,32]{0,1:T(8,128)S(1)}, u32[]{:S(2)}, u32[]{:S(2)}) collective-permute-start(f32[4096,32]{0,1:T(8,128)} %all-reduce.4.cloned.1.call-done), channel_id=1, source_target_pairs={{0,8},{8,0},{16,24},{24,16},{32,40},{40,32},{48,56},{56,48},{64,72... | collective-permute-start | bytes 1572872 | tf_op jit(solution)/shard_map/ppermute | solution.py:18
  340.0 5.7 copy-start.7
  340.0 406.4 %all-to-all-start = ((bf16[8,1,128,4096]{3,2,1,0:T(8,128)(2,1)}), bf16[8,1,128,4096]{3,2,1,0:T(8,128)(2,1)}, u32[]{:S(2)}, u32[]{:S(2)}) async-start(bf16[8,1,128,4096]{3,2,1,0:T(8,128)(2,1)} %stack.2), calls=%async_computation | async-start | bytes 16777216 | tf_op jit(solution)/shard_map/all_to_all | solution.py:28
  345.1 237.5 %all-reduce.6.cloned.1.call-start = ((), (), s32[]{:S(2)}) async-start(), calls=%async_computation.3 | async-start | bytes 1048576 | tf_op jit(solution)/shard_map/psum | solution.py:50
  355.0 3.2 copy-start.3
  363.3 53.0 %collective-permute-start.2 = (f32[512,32]{0,1:T(8,128)S(1)}, f32[512,32]{0,1:T(8,128)S(1)}, u32[]{:S(2)}, u32[]{:S(2)}) collective-permute-start(f32[512,32]{0,1:T(8,128)S(1)} %fusion.42), channel_id=1, source_target_pairs={{0,16},{16,0},{8,24},{24,8},{32,48},{48,32},{40,56},{56,40},{64,80... | collective-permute-start | bytes 196616 | tf_op jit(solution)/shard_map/ppermute | solution.py:18
  503.7 241.2 %all-reduce.8.cloned.1.call-start = ((), (), s32[]{:S(2)}) async-start(), calls=%async_computation.4 | async-start | bytes 1048576 | tf_op jit(solution)/shard_map/psum | solution.py:50
  582.6 10.9 %collective-permute-start.3 = (f32[4096,32]{0,1:T(8,128)}, f32[4096,32]{0,1:T(8,128)S(1)}, u32[]{:S(2)}, u32[]{:S(2)}) collective-permute-start(f32[4096,32]{0,1:T(8,128)} %all-reduce.6.cloned.1.call-done), channel_id=1, source_target_pairs={{0,16},{16,0},{8,24},{24,8},{32,48},{48,32},{40,56},{56,40},{64,80... | collective-permute-start | bytes 1572872 | tf_op jit(solution)/shard_map/ppermute | solution.py:18
  602.9 3.2 copy-start.2
  611.2 4.4 collective-permute-start.4
  744.8 11.7 %collective-permute-start.5 = (f32[4096,32]{0,1:T(8,128)}, f32[4096,32]{0,1:T(8,128)S(1)}, u32[]{:S(2)}, u32[]{:S(2)}) collective-permute-start(f32[4096,32]{0,1:T(8,128)} %all-reduce.8.cloned.1.call-done), channel_id=1, source_target_pairs={{0,32},{32,0},{8,40},{40,8},{16,48},{48,16},{24,56},{56,24},{64,96... | collective-permute-start | bytes 1572872 | tf_op jit(solution)/shard_map/ppermute | solution.py:18
  746.4 10.2 %copy-start.8 = (f32[4096,32]{0,1:T(8,128)S(1)}, f32[4096,32]{0,1:T(8,128)}, u32[]{:S(2)}) copy-start(f32[4096,32]{0,1:T(8,128)} %all-reduce.8.cloned.1.call-done) | copy-start | bytes 1572868
  746.4 20.8 %copy-start.1 = (bf16[1,1024,512]{2,1,0:T(8,128)(2,1)S(1)}, bf16[1,1024,512]{2,1,0:T(8,128)(2,1)}, u32[]{:S(2)}) copy-start(bf16[1,1024,512]{2,1,0:T(8,128)(2,1)} %param.9) | copy-start | bytes 3145732
Sparse Core Ops, SparseCore 0:
  9.8 173.3 all-gather.1
  257.1 78.5 all-reduce.3
  503.8 78.7 all-reduce.5
  666.2 78.5 all-reduce.7
